TPU v7x, 32 devices: a whole 2x2x4 slice. The times are simulated.
32 devices in a mesh: gx: 8 (over z, y), gy: 4 (over x, core).
Axes of the slice: x: 2, y: 2, z: 4, core: 2. Of those that a mesh axis runs over, the one named last changes fastest.
Arguments:
- conc_prev: float32 [128, 64, 128], P('gx', 'gy'), may hold values from 0.5 to 2
- right_side: float32 [128, 64, 128], P('gx', 'gy'), may hold values from -5 to 7
- soil_id: int32 [128, 64, 128], P('gx', 'gy'), may hold values from 0 to 7
- soil_table: float32 [5, 8], replicated, may hold values from 0.3 to 3
Outputs:
- correction: float32 [128, 64, 128], P('gx', 'gy')
All inputs are finite; a program needn't handle non-finite values.
Results may differ from a plain program's by a relative error of at most 0.00002.
Values sent between devices are 32-bit elements; how exact they have to be, the bound alone decides.
No kernel may reach another device: no remote copies, remote signals or barrier semaphores. Data moves between devices by JAX's collectives and lax.ppermute only.
A program may use at most 128 MiB of HBM per device.

v0:
```python
import jax
import jax.numpy as jnp
from jax import lax
from jax.sharding import PartitionSpec as P

CHEB = 3
COARSE_SWEEPS = 8
storage_scale = 0.05
cheb_centre = 1.1
cheb_half = 0.9
cheb_ratio = cheb_centre / cheb_half
jacobi_weight = 0.8


def padded_2(cells, sides, width):
    for axis, dim in sides:
        count = lax.axis_size(axis)
        ends = count - 1
        head = lax.slice_in_dim(cells, 0, width, axis=dim)
        tail = lax.slice_in_dim(cells, cells.shape[dim] - width, cells.shape[dim], axis=dim)
        cells = jnp.concatenate(
            [
                lax.ppermute(tail, axis, [(i, (i + 1) % count) for i in range(ends)]),
                cells,
                lax.ppermute(head, axis, [((i + 1) % count, i) for i in range(ends)]),
            ],
            axis=dim,
        )
    return cells


def harmonic(first, second):
    return first * second / jnp.maximum(0.5 * (first + second), 0.1)


def face_terms(coeffs, spacing):
    eastward = coeffs[0]
    northward = coeffs[1]
    upward = coeffs[2]
    centre_x = eastward[1:-1, 1:-1]
    centre_y = northward[1:-1, 1:-1]
    centre_z = upward[1:-1, 1:-1]
    east_face = harmonic(eastward[2:, 1:-1], centre_x) * spacing
    west_face = harmonic(eastward[:-2, 1:-1], centre_x) * spacing
    north_face = harmonic(northward[1:-1, 2:], centre_y) * spacing
    south_face = harmonic(northward[1:-1, :-2], centre_y) * spacing
    vertical = harmonic(centre_z[:, :, 1:], centre_z[:, :, :-1]) * spacing
    closed = jnp.zeros_like(centre_z[:, :, :1])
    above_face = jnp.concatenate([vertical, closed], axis=2)
    below_face = jnp.concatenate([closed, vertical], axis=2)
    storage = coeffs[3, 1:-1, 1:-1]
    return (east_face, west_face, north_face, south_face, above_face, below_face, storage)


def main_diagonal(coeffs, spacing):
    east_face, west_face, north_face, south_face, above_face, below_face, storage = face_terms(
        coeffs, spacing
    )
    return jnp.maximum(
        storage + east_face + west_face + north_face + south_face + above_face + below_face, 0.01
    )


def operate(values, coeffs, spacing):
    east_face, west_face, north_face, south_face, above_face, below_face, storage = face_terms(
        coeffs, spacing
    )
    centre = values[1:-1, 1:-1]
    upper_cell = jnp.concatenate([centre[:, :, 1:], centre[:, :, :1]], axis=2)
    lower_cell = jnp.concatenate([centre[:, :, -1:], centre[:, :, :-1]], axis=2)
    fluxes = east_face * (centre - values[2:, 1:-1]) + west_face * (centre - values[:-2, 1:-1])
    fluxes = (
        fluxes
        + north_face * (centre - values[1:-1, 2:])
        + south_face * (centre - values[1:-1, :-2])
    )
    fluxes = fluxes + above_face * (centre - upper_cell) + below_face * (centre - lower_cell)
    return storage * centre + fluxes


def coarsen(values):
    lead = values.shape[:-3]
    size_x, size_y, size_z = values.shape[-3:]
    split = values.reshape(lead + (size_x // 2, 2, size_y // 2, 2, size_z // 2, 2))
    return jnp.mean(split, axis=(-5, -3, -1))


def prolong(values):
    return jnp.repeat(jnp.repeat(jnp.repeat(values, 2, axis=0), 2, axis=1), 2, axis=2)


def shrink(values, amount):
    if amount == 0:
        return values
    return values[..., amount:-amount, amount:-amount, :]


def tile_halo(layers, amount):
    return padded_2(layers, (("gx", 1), ("gy", 2)), amount)


def expand(values):
    return (tile_halo(values[None], 1)[0], 1)


def smooth(target, target_margin, initial, coeffs, coeff_margin, spacing):
    if initial is None:
        current = target_margin
        diagonal = main_diagonal(shrink(coeffs, coeff_margin - current - 1), spacing)
        update = target / diagonal * (1.0 / cheb_centre)
        iterate = update
    else:
        padded, padded_margin = expand(initial)
        applied = operate(padded, shrink(coeffs, coeff_margin - padded_margin), spacing)
        current = padded_margin - 1
        diagonal = main_diagonal(shrink(coeffs, coeff_margin - current - 1), spacing)
        misfit = shrink(target, target_margin - current) - applied
        update = misfit / diagonal * (1.0 / cheb_centre)
        iterate = shrink(padded, 1) + update
    diagonal_margin = current
    factor = 1.0 / cheb_ratio
    for repeat in range(CHEB - 1):
        padded, padded_margin = expand(iterate)
        applied = operate(padded, shrink(coeffs, coeff_margin - padded_margin), spacing)
        next_margin = padded_margin - 1
        misfit = shrink(target, target_margin - next_margin) - applied
        factor_new = 1.0 / (2.0 * cheb_ratio - factor)
        update = factor_new * factor * shrink(
            update, current - next_margin
        ) + 2.0 * factor_new / cheb_half * (
            misfit / shrink(diagonal, diagonal_margin - next_margin)
        )
        iterate = shrink(iterate, current - next_margin) + update
        current = next_margin
        factor = factor_new
    return (iterate, current)


def leftover(target, target_margin, iterate, coeffs, coeff_margin, spacing):
    padded, padded_margin = expand(iterate)
    applied = operate(padded, shrink(coeffs, coeff_margin - padded_margin), spacing)
    return shrink(target, target_margin - padded_margin + 1) - applied


def local_fields(conc_prev, soil_id, soil_table):
    fields = []
    for record in range(5):
        looked = jnp.zeros(soil_id.shape, jnp.float32)
        for material in range(soil_table.shape[1]):
            looked = looked + jnp.where(soil_id == material, soil_table[record, material], 0.0)
        fields.append(looked)
    storage = storage_scale * (1.0 + fields[3] * jnp.exp((fields[4] - 1.0) * jnp.log(conc_prev)))
    return jnp.stack([fields[0], fields[1], fields[2], storage])


def local(conc_prev, right_side, soil_id, soil_table):
    halo_depth = 0
    fine_margin = max(4, 2 * halo_depth + 2)
    own_coeffs = local_fields(conc_prev, soil_id, soil_table)
    fine_coeffs = padded_2(own_coeffs, (("gx", 1), ("gy", 2)), fine_margin)
    mid_margin = fine_margin // 2
    mid_coeffs = coarsen(fine_coeffs)
    coarse_coeffs = coarsen(shrink(mid_coeffs, mid_margin - 2))
    fine_iterate, current = smooth(right_side, halo_depth, None, fine_coeffs, fine_margin, 1.0)
    fine_misfit = leftover(right_side, halo_depth, fine_iterate, fine_coeffs, fine_margin, 1.0)
    fine_iterate = shrink(fine_iterate, current)
    mid_plain = coarsen(fine_misfit)
    mid_iterate, current = smooth(mid_plain, halo_depth, None, mid_coeffs, mid_margin, 0.25)
    mid_misfit = leftover(mid_plain, halo_depth, mid_iterate, mid_coeffs, mid_margin, 0.25)
    mid_iterate = shrink(mid_iterate, current)
    coarse_source = coarsen(mid_misfit)
    narrow = coarse_coeffs[:, :, 1:-1]
    group_source, group_coeffs = (
        lax.all_gather(coarse_source, "gy", axis=1, tiled=True),
        lax.all_gather(narrow, "gy", axis=2, tiled=True),
    )
    line_total = jnp.sum(group_source, axis=1)
    line_store = jnp.sum(group_coeffs[3, 1:-1], axis=1)
    line_mean = line_total / line_store
    group_coeffs = jnp.pad(group_coeffs, ((0, 0), (0, 0), (1, 1), (0, 0)))
    diagonal = main_diagonal(group_coeffs, 0.0625)
    coarse_value = jnp.broadcast_to(line_mean[:, None, :], group_source.shape)
    for sweeps in range(COARSE_SWEEPS):
        padded = padded_2(coarse_value, (("gx", 0),), 1)
        padded = jnp.pad(padded, ((0, 0), (1, 1), (0, 0)))
        applied = operate(padded, group_coeffs, 0.0625)
        coarse_value = coarse_value + jacobi_weight * ((group_source - applied) / diagonal)
    tile_width = coarse_source.shape[1]
    coarse_value = lax.dynamic_slice_in_dim(
        coarse_value, lax.axis_index("gy") * tile_width, tile_width, 1
    )
    mid_start = mid_iterate + prolong(coarse_value)
    mid_result, current = smooth(mid_plain, halo_depth, mid_start, mid_coeffs, mid_margin, 0.25)
    fine_start = fine_iterate + prolong(mid_result)
    fine_result, current = smooth(right_side, halo_depth, fine_start, fine_coeffs, fine_margin, 1.0)
    return fine_result


def solution(mesh):
    placed = (P("gx", "gy", None), P("gx", "gy", None), P("gx", "gy", None), P())
    return jax.shard_map(
        local, mesh=mesh, in_specs=placed, out_specs=P("gx", "gy", None), check_vma=False
    )
```

profile of v0, /device:TPU:26, one launch (start us, length us, event | category | flops | bytes accessed | tf_op | source)
XLA Modules:
  0.0 402.7 jit_solution(15851466285160394497)
XLA Ops:
  5.6 6.3 %add_bitcast_fusion.3 = (f32[1,16,16,128]{3,2,1,0:T(8,128)S(1)}, pred[16,16,128]{2,1,0:T(8,128)(4,1)S(1)}, pred[16,16,128]{2,1,0:T(8,128)(4,1)S(1)}, pred[16,16,...) fusion(f32[]{:T(128)} %bitcast.23, f32[]{:T(128)} %bitcast.22, ...), kind=kLoop, calls=%fused_computation.162 | loop fusion | flops 753664 | bytes 524320 | tf_op jit(solution)/shard_map/stack | solution.py:153
  11.9 5.3 %add_bitcast_fusion.1 = f32[1,16,16,128]{3,2,1,0:T(8,128)S(1)} fusion(pred[16,16,128]{2,1,0:T(8,128)(4,1)S(1)} %get-tuple-element.49, pred[16,16,128]{2,1,0:T(8,128)(4,1)S(1)} %get-tuple-element.48, pred[16,16,128]{2,1,0:T(8,128)(4,1)S(1)} %get-tuple-element.47, pred[16,16,128]{2,1,0:T(8,128)(4,1)S(1)} %get-tuple-element.46, ...), kind=kLoop, calls=%fused_computation.160 | loop fusion | flops 491520 | bytes 393248 | tf_op jit(solution)/shard_map/stack | solution.py:153
  17.2 5.0 %add_bitcast_fusion.2 = f32[1,16,16,128]{3,2,1,0:T(8,128)S(1)} fusion(pred[16,16,128]{2,1,0:T(8,128)(4,1)S(1)} %get-tuple-element.49, pred[16,16,128]{2,1,0:T(8,128)(4,1)S(1)} %get-tuple-element.48, pred[16,16,128]{2,1,0:T(8,128)(4,1)S(1)} %get-tuple-element.47, pred[16,16,128]{2,1,0:T(8,128)(4,1)S(1)} %get-tuple-element.46, ...), kind=kLoop, calls=%fused_computation.161 | loop fusion | flops 491520 | bytes 393248 | tf_op jit(solution)/shard_map/stack | solution.py:153
  22.1 10.1 %add_multiply_fusion = f32[16,16,128]{2,1,0:T(8,128)S(1)} fusion(f32[16,16,128]{2,1,0:T(8,128)S(1)} %copy-done.1, pred[16,16,128]{2,1,0:T(8,128)(4,1)S(1)} %get-tuple-element.49, pred[16,16,128]{2,1,0:T(8,128)(4,1)S(1)} %get-tuple-element.48, pred[16,16,128]{2,1,0:T(8,128)(4,1)S(1)} %get-tuple-element.47, pred[16,16,128]{2,1,0:T(8,128)(4,1)S(1)} %get-tuple-element.46, ...), kind=kLoop, calls=%fused_computation.163 | loop fusion | flops 1146880 | bytes 524352 | tf_op jit(solution)/shard_map/mul | solution.py:152
  39.5 4.0 collective-permute-done
  72.8 3.9 collective-permute-start.8
  76.7 18.2 %copy.868 = f32[4,24,24,128]{0,3,2,1:T(8,128)} copy(f32[4,24,24,128]{3,2,1,0:T(8,128)S(1)} %pad_maximum_fusion) | data formatting | bytes 2359296 | tf_op jit(solution)/shard_map/concatenate | solution.py:21
  94.9 27.0 %reduce_sum.55 = f32[4,12,12,64]{0,3,2,1:T(8,128)} reduce(f32[4,12,2,12,2,64,2]{0,6,5,4,3,2,1:T(2,128)} %bitcast.161, f32[]{:T(128)} %constant.27.clone.1), dimensions={2,4,6}, to_apply=%region_1.2 | reduce | flops 258048 | bytes 1327108 | tf_op jit(solution)/shard_map/reduce_sum | solution.py:85
  149.8 9.8 %reshape.56 = f32[8,2,8,2,64,2]{5,4,3,2,1,0:T(8,128)} reshape(f32[16,16,128]{2,1,0:T(8,128)S(1)} %fusion.41) | data formatting | bytes 262144 | tf_op jit(solution)/shard_map/reshape | solution.py:84
  159.6 4.0 reduce_sum.54
  165.7 4.0 collective-permute-start.16
  172.8 5.3 %reduce_sum.58 = f32[4,6,6,32]{0,3,2,1:T(8,128)S(1)} reduce(f32[4,6,2,6,2,32,2]{0,6,5,4,3,2,1:T(2,128)} %bitcast.162, f32[]{:T(128)} %constant.27.clone.1), dimensions={2,4,6}, to_apply=%region_4.5 | reduce | flops 32256 | bytes 165892 | tf_op jit(solution)/shard_map/reduce_sum | solution.py:85
  191.3 10.7 %all_gather.7 = f32[4,6,16,32]{0,3,2,1:T(8,128)S(1)} all-gather(f32[4,6,4,32]{0,3,2,1:T(8,128)S(1)} %slice_multiply_fusion), channel_id=1, replica_groups=mesh['gx'=8,'gy'=4] {'gy'}, dimensions={2}, use_global_device_ids=true | all-gather | bytes 61440 | tf_op jit(solution)/shard_map/all_gather | solution.py:175
  202.0 4.6 %collective-permute-start.23 = (f32[1,10,1,64]{3,2,1,0:T(1,128)S(1)}, f32[1,10,1,64]{3,2,1,0:T(1,128)S(1)}, u32[]{:S(2)}, u32[]{:S(2)}) collective-permute-start(f32[1,10,1,64]{3,2,1,0:T(1,128)S(1)} %get-tuple-element.143), channel_id=1, source_target_pairs={{1,0},{2,1},{3,2},{5,4},{6,5},{7,6},{9,8},{10,9},{11,10},{13,12},{... | collective-permute-start | bytes 7688 | tf_op jit(solution)/shard_map/ppermute | solution.py:25
  217.9 4.3 %collective-permute-done.24 = f32[1,1,8,64]{3,2,1,0:T(8,128)S(1)} collective-permute-done((f32[1,1,8,64]{3,2,1,0:T(8,128)S(1)}, f32[1,1,8,64]{3,2,1,0:T(8,128)S(1)}, u32[]{:S(2)}, u32[]{:S(2)}) %collective-permute-start.24) | collective-permute-done | bytes 2080 | tf_op jit(solution)/shard_map/ppermute | solution.py:23
  230.6 5.2 %all_gather.6 = f32[4,16,32]{2,0,1:T(4,128)S(1)} all-gather(f32[4,4,32]{2,0,1:T(4,128)S(1)} %copy.879), channel_id=1, replica_groups=mesh['gx'=8,'gy'=4] {'gy'}, dimensions={1}, use_global_device_ids=true | all-gather | bytes 10240 | tf_op jit(solution)/shard_map/all_gather | solution.py:174
  237.9 3.9 collective-permute-start.29
  256.2 3.9 collective-permute-start.33
  274.2 3.9 collective-permute-start.37
  300.1 3.9 collective-permute-start.43
  309.0 3.9 collective-permute-start.44
  324.5 3.9 collective-permute-start.48
  356.6 3.9 collective-permute-start.56
  372.4 3.9 collective-permute-start.60
  (303 shorter events, 242.2 us)
Async XLA Ops:
  32.3 7.1 %collective-permute-start.1 = (f32[4,4,16,128]{3,2,1,0:T(8,128)S(1)}, f32[4,4,16,128]{3,2,1,0:T(8,128)S(1)}, u32[]{:S(2)}, u32[]{:S(2)}) collective-permute-start(f32[4,4,16,128]{3,2,1,0:T(8,128)S(1)} %get-tuple-element.56), channel_id=1, source_target_pairs={{4,0},{8,4},{12,8},{16,12},{20,16},{24,20},{28,24},{5,1},{9,5},{13... | collective-permute-start | bytes 393224 | tf_op jit(solution)/shard_map/ppermute | solution.py:25
  35.6 7.8 %collective-permute-start = (f32[4,4,16,128]{3,2,1,0:T(8,128)S(1)}, f32[4,4,16,128]{3,2,1,0:T(8,128)S(1)}, u32[]{:S(2)}, u32[]{:S(2)}) collective-permute-start(f32[4,4,16,128]{3,2,1,0:T(8,128)S(1)} %get-tuple-element.55), channel_id=1, source_target_pairs={{0,4},{4,8},{8,12},{12,16},{16,20},{20,24},{24,28},{1,5},{5,9},{9,... | collective-permute-start | bytes 393224 | tf_op jit(solution)/shard_map/ppermute | solution.py:23
  45.5 7.0 %collective-permute-start.2 = (f32[4,24,4,128]{3,1,2,0:T(8,128)S(1)}, f32[4,24,4,128]{3,1,2,0:T(8,128)S(1)}, u32[]{:S(2)}, u32[]{:S(2)}) collective-permute-start(f32[4,24,4,128]{3,1,2,0:T(8,128)S(1)} %copy.912), channel_id=1, source_target_pairs={{0,1},{1,2},{2,3},{4,5},{5,6},{6,7},{8,9},{9,10},{10,11},{12,13},{... | collective-permute-start | bytes 589832 | tf_op jit(solution)/shard_map/ppermute | solution.py:23
  57.0 6.4 %collective-permute-start.4 = (f32[1,1,16,128]{3,2,1,0:T(8,128)S(1)}, f32[1,1,16,128]{3,2,1,0:T(8,128)S(1)}, u32[]{:S(2)}, u32[]{:S(2)}) collective-permute-start(f32[1,1,16,128]{3,2,1,0:T(8,128)S(1)} %get-tuple-element.108), channel_id=1, source_target_pairs={{0,4},{4,8},{8,12},{12,16},{16,20},{20,24},{24,28},{1,5},{5,9},{9,... | collective-permute-start | bytes 24584 | tf_op jit(solution)/shard_map/ppermute | solution.py:23
  70.9 54.8 %collective-permute-start.9 = (f32[1,1,16,128]{3,2,1,0:T(8,128)S(1)}, f32[1,1,16,128]{3,2,1,0:T(8,128)S(1)}, u32[]{:S(2)}, u32[]{:S(2)}) collective-permute-start(f32[1,1,16,128]{3,2,1,0:T(8,128)S(1)} %get-tuple-element.107), channel_id=1, source_target_pairs={{4,0},{8,4},{12,8},{16,12},{20,16},{24,20},{28,24},{5,1},{9,5},{13... | collective-permute-start | bytes 24584 | tf_op jit(solution)/shard_map/ppermute | solution.py:25
  72.8 52.9 %collective-permute-start.8 = (f32[1,1,16,128]{3,2,1,0:T(8,128)S(1)}, f32[1,1,16,128]{3,2,1,0:T(8,128)S(1)}, u32[]{:S(2)}, u32[]{:S(2)}) collective-permute-start(f32[1,1,16,128]{3,2,1,0:T(8,128)S(1)} %get-tuple-element.106), channel_id=1, source_target_pairs={{0,4},{4,8},{8,12},{12,16},{16,20},{20,24},{24,28},{1,5},{5,9},{9,... | collective-permute-start | bytes 24584 | tf_op jit(solution)/shard_map/ppermute | solution.py:23
  136.0 6.4 %collective-permute-start.12 = (f32[1,1,16,128]{3,2,1,0:T(8,128)S(1)}, f32[1,1,16,128]{3,2,1,0:T(8,128)S(1)}, u32[]{:S(2)}, u32[]{:S(2)}) collective-permute-start(f32[1,1,16,128]{3,2,1,0:T(8,128)S(1)} %get-tuple-element.104), channel_id=1, source_target_pairs={{0,4},{4,8},{8,12},{12,16},{16,20},{20,24},{24,28},{1,5},{5,9},{9,... | collective-permute-start | bytes 24584 | tf_op jit(solution)/shard_map/ppermute | solution.py:23
  163.7 14.5 %collective-permute-start.17 = (f32[1,1,8,64]{3,2,1,0:T(8,128)S(1)}, f32[1,1,8,64]{3,2,1,0:T(8,128)S(1)}, u32[]{:S(2)}, u32[]{:S(2)}) collective-permute-start(f32[1,1,8,64]{3,2,1,0:T(8,128)S(1)} %get-tuple-element.201), channel_id=1, source_target_pairs={{4,0},{8,4},{12,8},{16,12},{20,16},{24,20},{28,24},{5,1},{9,5},{13... | collective-permute-start | bytes 6152 | tf_op jit(solution)/shard_map/ppermute | solution.py:25
  165.7 12.5 %collective-permute-start.16 = (f32[1,1,8,64]{3,2,1,0:T(8,128)S(1)}, f32[1,1,8,64]{3,2,1,0:T(8,128)S(1)}, u32[]{:S(2)}, u32[]{:S(2)}) collective-permute-start(f32[1,1,8,64]{3,2,1,0:T(8,128)S(1)} %get-tuple-element.200), channel_id=1, source_target_pairs={{0,4},{4,8},{8,12},{12,16},{16,20},{20,24},{24,28},{1,5},{5,9},{9,... | collective-permute-start | bytes 6152 | tf_op jit(solution)/shard_map/ppermute | solution.py:23
  185.5 16.6 %collective-permute-start.21 = (f32[1,1,8,64]{3,2,1,0:T(8,128)S(1)}, f32[1,1,8,64]{3,2,1,0:T(8,128)S(1)}, u32[]{:S(2)}, u32[]{:S(2)}) collective-permute-start(f32[1,1,8,64]{3,2,1,0:T(8,128)S(1)} %get-tuple-element.199), channel_id=1, source_target_pairs={{4,0},{8,4},{12,8},{16,12},{20,16},{24,20},{28,24},{5,1},{9,5},{13... | collective-permute-start | bytes 6152 | tf_op jit(solution)/shard_map/ppermute | solution.py:25
  188.4 13.6 %collective-permute-start.20 = (f32[1,1,8,64]{3,2,1,0:T(8,128)S(1)}, f32[1,1,8,64]{3,2,1,0:T(8,128)S(1)}, u32[]{:S(2)}, u32[]{:S(2)}) collective-permute-start(f32[1,1,8,64]{3,2,1,0:T(8,128)S(1)} %get-tuple-element.198), channel_id=1, source_target_pairs={{0,4},{4,8},{8,12},{12,16},{16,20},{20,24},{24,28},{1,5},{5,9},{9,... | collective-permute-start | bytes 6152 | tf_op jit(solution)/shard_map/ppermute | solution.py:23
  202.0 8.8 %collective-permute-start.23 = (f32[1,10,1,64]{3,2,1,0:T(1,128)S(1)}, f32[1,10,1,64]{3,2,1,0:T(1,128)S(1)}, u32[]{:S(2)}, u32[]{:S(2)}) collective-permute-start(f32[1,10,1,64]{3,2,1,0:T(1,128)S(1)} %get-tuple-element.143), channel_id=1, source_target_pairs={{1,0},{2,1},{3,2},{5,4},{6,5},{7,6},{9,8},{10,9},{11,10},{13,12},{... | collective-permute-start | bytes 7688 | tf_op jit(solution)/shard_map/ppermute | solution.py:25
  215.7 6.4 %collective-permute-start.24 = (f32[1,1,8,64]{3,2,1,0:T(8,128)S(1)}, f32[1,1,8,64]{3,2,1,0:T(8,128)S(1)}, u32[]{:S(2)}, u32[]{:S(2)}) collective-permute-start(f32[1,1,8,64]{3,2,1,0:T(8,128)S(1)} %get-tuple-element.196), channel_id=1, source_target_pairs={{0,4},{4,8},{8,12},{12,16},{16,20},{20,24},{24,28},{1,5},{5,9},{9,... | collective-permute-start | bytes 6152 | tf_op jit(solution)/shard_map/ppermute | solution.py:23
  237.9 6.4 %collective-permute-start.29 = (f32[1,16,32]{2,1,0:T(8,128)S(1)}, f32[1,16,32]{2,1,0:T(8,128)S(1)}, u32[]{:S(2)}, u32[]{:S(2)}) collective-permute-start(f32[1,16,32]{2,1,0:T(8,128)S(1)} %broadcast_in_dim.285), channel_id=1, source_target_pairs={{0,4},{4,8},{8,12},{12,16},{16,20},{20,24},{24,28},{1,5},{5,9},{9,... | collective-permute-start | bytes 6152 | tf_op jit(solution)/shard_map/ppermute | solution.py:23
  247.6 6.4 %collective-permute-start.31 = (f32[1,16,32]{2,1,0:T(8,128)S(1)}, f32[1,16,32]{2,1,0:T(8,128)S(1)}, u32[]{:S(2)}, u32[]{:S(2)}) collective-permute-start(f32[1,16,32]{2,1,0:T(8,128)S(1)} %get-tuple-element.190), channel_id=1, source_target_pairs={{0,4},{4,8},{8,12},{12,16},{16,20},{20,24},{24,28},{1,5},{5,9},{9,... | collective-permute-start | bytes 6152 | tf_op jit(solution)/shard_map/ppermute | solution.py:23
  256.2 6.4 %collective-permute-start.33 = (f32[1,16,32]{2,1,0:T(8,128)S(1)}, f32[1,16,32]{2,1,0:T(8,128)S(1)}, u32[]{:S(2)}, u32[]{:S(2)}) collective-permute-start(f32[1,16,32]{2,1,0:T(8,128)S(1)} %get-tuple-element.184), channel_id=1, source_target_pairs={{0,4},{4,8},{8,12},{12,16},{16,20},{20,24},{24,28},{1,5},{5,9},{9,... | collective-permute-start | bytes 6152 | tf_op jit(solution)/shard_map/ppermute | solution.py:23
  265.7 6.4 %collective-permute-start.35 = (f32[1,16,32]{2,1,0:T(8,128)S(1)}, f32[1,16,32]{2,1,0:T(8,128)S(1)}, u32[]{:S(2)}, u32[]{:S(2)}) collective-permute-start(f32[1,16,32]{2,1,0:T(8,128)S(1)} %get-tuple-element.178), channel_id=1, source_target_pairs={{0,4},{4,8},{8,12},{12,16},{16,20},{20,24},{24,28},{1,5},{5,9},{9,... | collective-permute-start | bytes 6152 | tf_op jit(solution)/shard_map/ppermute | solution.py:23
  274.2 6.4 %collective-permute-start.37 = (f32[1,16,32]{2,1,0:T(8,128)S(1)}, f32[1,16,32]{2,1,0:T(8,128)S(1)}, u32[]{:S(2)}, u32[]{:S(2)}) collective-permute-start(f32[1,16,32]{2,1,0:T(8,128)S(1)} %get-tuple-element.172), channel_id=1, source_target_pairs={{0,4},{4,8},{8,12},{12,16},{16,20},{20,24},{24,28},{1,5},{5,9},{9,... | collective-permute-start | bytes 6152 | tf_op jit(solution)/shard_map/ppermute | solution.py:23
  282.8 6.4 %collective-permute-start.39 = (f32[1,16,32]{2,1,0:T(8,128)S(1)}, f32[1,16,32]{2,1,0:T(8,128)S(1)}, u32[]{:S(2)}, u32[]{:S(2)}) collective-permute-start(f32[1,16,32]{2,1,0:T(8,128)S(1)} %get-tuple-element.166), channel_id=1, source_target_pairs={{0,4},{4,8},{8,12},{12,16},{16,20},{20,24},{24,28},{1,5},{5,9},{9,... | collective-permute-start | bytes 6152 | tf_op jit(solution)/shard_map/ppermute | solution.py:23
  291.4 6.4 %collective-permute-start.41 = (f32[1,16,32]{2,1,0:T(8,128)S(1)}, f32[1,16,32]{2,1,0:T(8,128)S(1)}, u32[]{:S(2)}, u32[]{:S(2)}) collective-permute-start(f32[1,16,32]{2,1,0:T(8,128)S(1)} %get-tuple-element.160), channel_id=1, source_target_pairs={{0,4},{4,8},{8,12},{12,16},{16,20},{20,24},{24,28},{1,5},{5,9},{9,... | collective-permute-start | bytes 6152 | tf_op jit(solution)/shard_map/ppermute | solution.py:23
  300.1 6.4 %collective-permute-start.43 = (f32[1,16,32]{2,1,0:T(8,128)S(1)}, f32[1,16,32]{2,1,0:T(8,128)S(1)}, u32[]{:S(2)}, u32[]{:S(2)}) collective-permute-start(f32[1,16,32]{2,1,0:T(8,128)S(1)} %get-tuple-element.158), channel_id=1, source_target_pairs={{0,4},{4,8},{8,12},{12,16},{16,20},{20,24},{24,28},{1,5},{5,9},{9,... | collective-permute-start | bytes 6152 | tf_op jit(solution)/shard_map/ppermute | solution.py:23
  356.6 6.4 %collective-permute-start.56 = (f32[1,1,16,128]{3,2,1,0:T(8,128)S(1)}, f32[1,1,16,128]{3,2,1,0:T(8,128)S(1)}, u32[]{:S(2)}, u32[]{:S(2)}) collective-permute-start(f32[1,1,16,128]{3,2,1,0:T(8,128)S(1)} %get-tuple-element.102), channel_id=1, source_target_pairs={{0,4},{4,8},{8,12},{12,16},{16,20},{20,24},{24,28},{1,5},{5,9},{9,... | collective-permute-start | bytes 24584 | tf_op jit(solution)/shard_map/ppermute | solution.py:23
  372.4 6.4 %collective-permute-start.60 = (f32[1,1,16,128]{3,2,1,0:T(8,128)S(1)}, f32[1,1,16,128]{3,2,1,0:T(8,128)S(1)}, u32[]{:S(2)}, u32[]{:S(2)}) collective-permute-start(f32[1,1,16,128]{3,2,1,0:T(8,128)S(1)} %get-tuple-element.100), channel_id=1, source_target_pairs={{0,4},{4,8},{8,12},{12,16},{16,20},{20,24},{24,28},{1,5},{5,9},{9,... | collective-permute-start | bytes 24584 | tf_op jit(solution)/shard_map/ppermute | solution.py:23
  388.2 6.4 %collective-permute-start.64 = (f32[1,1,16,128]{3,2,1,0:T(8,128)S(1)}, f32[1,1,16,128]{3,2,1,0:T(8,128)S(1)}, u32[]{:S(2)}, u32[]{:S(2)}) collective-permute-start(f32[1,1,16,128]{3,2,1,0:T(8,128)S(1)} %get-tuple-element.98), channel_id=1, source_target_pairs={{0,4},{4,8},{8,12},{12,16},{16,20},{20,24},{24,28},{1,5},{5,9},{9,... | collective-permute-start | bytes 24584 | tf_op jit(solution)/shard_map/ppermute | solution.py:23
  (46 other events, 256.1 us)
where the time goes:
time: 405 us; the launch traced here: 403 us
  starting transfers between devices  181 us (45%)
  waiting for transfers between devices  85.1 us (21%)
  other arithmetic  69.4 us (17%)
  local copies, waits for them, and re-layouts  49.5 us (12%)
  blocking collectives  15.9 us (4%)
    ppermute x34, starting transfers between devices, padded_2(): lax.ppermute(tail, axis, [(i, (i + 1) % count) for i in range(ends)])  105 us
    ppermute x34, waiting for transfers between devices, padded_2(): lax.ppermute(tail, axis, [(i, (i + 1) % count) for i in range(ends)])  83 us
    ppermute x34, starting transfers between devices, padded_2(): lax.ppermute(head, axis, [((i + 1) % count, i) for i in range(ends)])  76.4 us
    reduce_sum x4, other arithmetic, coarsen(): return jnp.mean(split, axis=(-5, -3, -1))  36.5 us
    concatenate x1, local copies, waits for them, and re-layouts, padded_2(): jnp.concatenate([lax.ppermute(tail, axis, [(i, (i + 1) % count) for i in...  18.2 us
    another operation x3, other arithmetic, local_fields(): return jnp.stack([fields[0], fields[1], fields[2], storage])  16.5 us
    reshape x2, local copies, waits for them, and re-layouts, coarsen(): values.reshape(lead + (size_x // 2, 2, size_y // 2, 2, size_z // 2, 2))  10.9 us
    all_gather x1, blocking collectives, local(): lax.all_gather(narrow, 'gy', axis=2, tiled=True)  10.7 us
  transfers between devices with their start and end apart: 68, of which 33 were waited for; matrix products, arithmetic and copies ran while one was open for 15% of the time, Pallas kernels for 0%

commit v1 on v0

--- a/solution.py
+++ b/solution.py
@@ -2,6 +2,7 @@
 import jax.numpy as jnp
 from jax import lax
 from jax.sharding import PartitionSpec as P
+from jax.lax import axis_index, axis_size, ppermute
 
 CHEB = 3
 COARSE_SWEEPS = 8
@@ -10,6 +11,14 @@
 cheb_half = 0.9
 cheb_ratio = cheb_centre / cheb_half
 jacobi_weight = 0.8
+
+
+def recast_body(local_values, dim_i):
+    local_values = jnp.moveaxis(local_values, 0, dim_i)
+    heard = local_values.shape
+    return local_values.reshape(
+        *heard[:dim_i], heard[dim_i] * heard[dim_i + 1], *heard[dim_i + 2 :]
+    )
 
 
 def padded_2(cells, sides, width):
@@ -170,9 +179,27 @@
     mid_iterate = shrink(mid_iterate, current)
     coarse_source = coarsen(mid_misfit)
     narrow = coarse_coeffs[:, :, 1:-1]
+
+    def obtain_seats_all_here(here_x, chip_axis, dim_k):
+        slots = axis_size(chip_axis)
+        seen = [(rr, (rr + 1) % slots) for rr in range(slots)]
+        bank = [(dd, it) for it, dd in seen]
+        t_next, view_out = ([], [])
+        q = 0
+        while q < slots - 1:
+            if q % 2 == 0:
+                t_next.append(ppermute(t_next[-1] if t_next else here_x, chip_axis, seen))
+            else:
+                view_out.append(ppermute(view_out[-1] if view_out else here_x, chip_axis, bank))
+            q += 1
+        long_array = jnp.stack([*t_next[::-1], here_x, *view_out], axis=0)
+        x_now = axis_index(chip_axis) - len(t_next)
+        long_array = long_array[(jnp.arange(slots) - x_now) % slots]
+        return recast_body(long_array, dim_k)
+
     group_source, group_coeffs = (
         lax.all_gather(coarse_source, "gy", axis=1, tiled=True),
-        lax.all_gather(narrow, "gy", axis=2, tiled=True),
+        obtain_seats_all_here(narrow, "gy", 2),
     )
     line_total = jnp.sum(group_source, axis=1)
     line_store = jnp.sum(group_coeffs[3, 1:-1], axis=1)

time: 405 us -> 393 us (0.970)
  blocking collectives: 15.9 us -> 5.19 us
    all_gather x1 -> x0, blocking collectives: 10.7 us -> none  [local(): lax.all_gather(narrow, 'gy', axis=2, tiled=True)]
    ppermute x34, starting transfers between devices: 76.4 us -> 71.1 us  [padded_2(): lax.ppermute(head, axis, [((i + 1) % count, i) for i in range(ends)])]
  transfers between devices with their start and end apart: 68 -> 71, of which waited for: 33 -> 34; matrix products, arithmetic and copies ran while one was open for 15% -> 15% of each run, Pallas kernels for 0% -> 0%
where the time goes in v1:
time: 393 us; the launch traced here: 390 us
  starting transfers between devices  181 us (46%)
  waiting for transfers between devices  86.3 us (22%)
  other arithmetic  68.6 us (17%)
  local copies, waits for them, and re-layouts  47.8 us (12%)
  blocking collectives  5.19 us (1%)
    ppermute x34, starting transfers between devices, padded_2(): lax.ppermute(tail, axis, [(i, (i + 1) % count) for i in range(ends)])  108 us
    ppermute x34, waiting for transfers between devices, padded_2(): lax.ppermute(tail, axis, [(i, (i + 1) % count) for i in range(ends)])  84.2 us
    ppermute x34, starting transfers between devices, padded_2(): lax.ppermute(head, axis, [((i + 1) % count, i) for i in range(ends)])  71.1 us
    reduce_sum x4, other arithmetic, coarsen(): return jnp.mean(split, axis=(-5, -3, -1))  36.6 us
    concatenate x1, local copies, waits for them, and re-layouts, padded_2(): jnp.concatenate([lax.ppermute(tail, axis, [(i, (i + 1) % count) for i in...  17.9 us
    another operation x3, other arithmetic, local_fields(): return jnp.stack([fields[0], fields[1], fields[2], storage])  16.1 us
    reshape x2, local copies, waits for them, and re-layouts, coarsen(): values.reshape(lead + (size_x // 2, 2, size_y // 2, 2, size_z // 2, 2))  10.8 us
    mul x1, other arithmetic, local_fields(): storage_scale * (1.0 + fields[3] * jnp.exp((fields[4] - 1.0) * jnp.log(co...  10.4 us
  transfers between devices with their start and end apart: 71, of which 34 were waited for; matrix products, arithmetic and copies ran while one was open for 15% of the time, Pallas kernels for 0%

profile of v1, /device:TPU:26, one launch (start us, length us, event | category | flops | bytes accessed | tf_op | source)
XLA Modules:
  0.0 390.0 jit_solution(3949715331509523406)
XLA Ops:
  5.5 6.0 %add_bitcast_fusion.3 = (f32[1,16,16,128]{3,2,1,0:T(8,128)S(1)}, pred[16,16,128]{2,1,0:T(8,128)(4,1)S(1)}, pred[16,16,128]{2,1,0:T(8,128)(4,1)S(1)}, pred[16,16,...) fusion(f32[]{:T(128)} %bitcast.23, f32[]{:T(128)} %bitcast.22, ...), kind=kLoop, calls=%fused_computation.161 | loop fusion | flops 753664 | bytes 524320 | tf_op jit(solution)/shard_map/stack | solution.py:162
  11.5 5.1 %add_bitcast_fusion.1 = f32[1,16,16,128]{3,2,1,0:T(8,128)S(1)} fusion(pred[16,16,128]{2,1,0:T(8,128)(4,1)S(1)} %get-tuple-element.44, pred[16,16,128]{2,1,0:T(8,128)(4,1)S(1)} %get-tuple-element.43, pred[16,16,128]{2,1,0:T(8,128)(4,1)S(1)} %get-tuple-element.42, pred[16,16,128]{2,1,0:T(8,128)(4,1)S(1)} %get-tuple-element.41, ...), kind=kLoop, calls=%fused_computation.159 | loop fusion | flops 491520 | bytes 393248 | tf_op jit(solution)/shard_map/stack | solution.py:162
  16.6 5.1 %add_bitcast_fusion.2 = f32[1,16,16,128]{3,2,1,0:T(8,128)S(1)} fusion(pred[16,16,128]{2,1,0:T(8,128)(4,1)S(1)} %get-tuple-element.44, pred[16,16,128]{2,1,0:T(8,128)(4,1)S(1)} %get-tuple-element.43, pred[16,16,128]{2,1,0:T(8,128)(4,1)S(1)} %get-tuple-element.42, pred[16,16,128]{2,1,0:T(8,128)(4,1)S(1)} %get-tuple-element.41, ...), kind=kLoop, calls=%fused_computation.160 | loop fusion | flops 491520 | bytes 393248 | tf_op jit(solution)/shard_map/stack | solution.py:162
  21.7 10.4 %add_multiply_fusion = f32[16,16,128]{2,1,0:T(8,128)S(1)} fusion(f32[16,16,128]{2,1,0:T(8,128)S(1)} %copy-done.1, pred[16,16,128]{2,1,0:T(8,128)(4,1)S(1)} %get-tuple-element.44, pred[16,16,128]{2,1,0:T(8,128)(4,1)S(1)} %get-tuple-element.43, pred[16,16,128]{2,1,0:T(8,128)(4,1)S(1)} %get-tuple-element.42, pred[16,16,128]{2,1,0:T(8,128)(4,1)S(1)} %get-tuple-element.41, ...), kind=kLoop, calls=%fused_computation.162 | loop fusion | flops 1146880 | bytes 524352 | tf_op jit(solution)/shard_map/mul | solution.py:161
  39.2 4.0 %collective-permute-done = f32[4,4,16,128]{3,2,1,0:T(8,128)S(1)} collective-permute-done((f32[4,4,16,128]{3,2,1,0:T(8,128)S(1)}, f32[4,4,16,128]{3,2,1,0:T(8,128)S(1)}, u32[]{:S(2)}, u32[]{:S(2)}) %collective-permute-start) | collective-permute-done | bytes 131104 | tf_op jit(solution)/shard_map/ppermute | solution.py:32
  72.6 3.9 %collective-permute-start.8 = (f32[1,1,16,128]{3,2,1,0:T(8,128)S(1)}, f32[1,1,16,128]{3,2,1,0:T(8,128)S(1)}, u32[]{:S(2)}, u32[]{:S(2)}) collective-permute-start(f32[1,1,16,128]{3,2,1,0:T(8,128)S(1)} %get-tuple-element.106), channel_id=1, source_target_pairs={{0,4},{4,8},{8,12},{12,16},{16,20},{20,24},{24,28},{1,5},{5,9},{9,... | collective-permute-start | bytes 24584 | tf_op jit(solution)/shard_map/ppermute | solution.py:32
  76.5 17.9 %copy.584 = f32[4,24,24,128]{0,3,2,1:T(8,128)} copy(f32[4,24,24,128]{3,2,1,0:T(8,128)S(1)} %pad_maximum_fusion) | data formatting | bytes 2359296 | tf_op jit(solution)/shard_map/concatenate | solution.py:30
  94.5 27.0 %reduce_sum.55 = f32[4,12,12,64]{0,3,2,1:T(8,128)} reduce(f32[4,12,2,12,2,64,2]{0,6,5,4,3,2,1:T(2,128)} %bitcast.194, f32[]{:T(128)} %constant.28.clone.1), dimensions={2,4,6}, to_apply=%region_1.2 | reduce | flops 258048 | bytes 1327108 | tf_op jit(solution)/shard_map/reduce_sum | solution.py:94
  149.7 5.3 %reduce_sum.58 = f32[4,6,6,32]{0,3,2,1:T(8,128)S(1)} reduce(f32[4,6,2,6,2,32,2]{0,6,5,4,3,2,1:T(2,128)} %bitcast.195, f32[]{:T(128)} %constant.28.clone.1), dimensions={2,4,6}, to_apply=%region_4.5 | reduce | flops 32256 | bytes 165892 | tf_op jit(solution)/shard_map/reduce_sum | solution.py:94
  155.8 9.8 %reshape.108 = f32[8,2,8,2,64,2]{5,4,3,2,1,0:T(8,128)} reshape(f32[16,16,128]{2,1,0:T(8,128)S(1)} %fusion.41) | data formatting | bytes 262144 | tf_op jit(solution)/shard_map/reshape | solution.py:93
  165.5 4.0 %reduce_sum.54 = f32[8,8,64]{2,1,0:T(8,128)S(1)} reduce(f32[8,2,8,2,64,2]{5,4,3,2,1,0:T(8,128)} %reshape.108, f32[]{:T(128)} %constant.28.clone.1), dimensions={1,3,5}, to_apply=%region_0.1 | reduce | flops 28672 | bytes 147460 | tf_op jit(solution)/shard_map/reduce_sum | solution.py:94
  171.7 3.8 collective-permute-start.16
  218.7 5.2 %all_gather.3 = f32[4,16,32]{2,0,1:T(4,128)S(1)} all-gather(f32[4,4,32]{2,0,1:T(4,128)S(1)} %copy.595), channel_id=1, replica_groups=mesh['gx'=8,'gy'=4] {'gy'}, dimensions={1}, use_global_device_ids=true | all-gather | bytes 10240 | tf_op jit(solution)/shard_map/all_gather | solution.py:201
  253.0 3.9 %collective-permute-start.38 = (f32[1,16,32]{2,1,0:T(8,128)S(1)}, f32[1,16,32]{2,1,0:T(8,128)S(1)}, u32[]{:S(2)}, u32[]{:S(2)}) collective-permute-start(f32[1,16,32]{2,1,0:T(8,128)S(1)} %get-tuple-element.180), channel_id=1, source_target_pairs={{0,4},{4,8},{8,12},{12,16},{16,20},{20,24},{24,28},{1,5},{5,9},{9,... | collective-permute-start | bytes 6152 | tf_op jit(solution)/shard_map/ppermute | solution.py:32
  261.6 3.9 %collective-permute-start.40 = (f32[1,16,32]{2,1,0:T(8,128)S(1)}, f32[1,16,32]{2,1,0:T(8,128)S(1)}, u32[]{:S(2)}, u32[]{:S(2)}) collective-permute-start(f32[1,16,32]{2,1,0:T(8,128)S(1)} %get-tuple-element.174), channel_id=1, source_target_pairs={{0,4},{4,8},{8,12},{12,16},{16,20},{20,24},{24,28},{1,5},{5,9},{9,... | collective-permute-start | bytes 6152 | tf_op jit(solution)/shard_map/ppermute | solution.py:32
  270.1 3.9 %collective-permute-start.42 = (f32[1,16,32]{2,1,0:T(8,128)S(1)}, f32[1,16,32]{2,1,0:T(8,128)S(1)}, u32[]{:S(2)}, u32[]{:S(2)}) collective-permute-start(f32[1,16,32]{2,1,0:T(8,128)S(1)} %get-tuple-element.168), channel_id=1, source_target_pairs={{0,4},{4,8},{8,12},{12,16},{16,20},{20,24},{24,28},{1,5},{5,9},{9,... | collective-permute-start | bytes 6152 | tf_op jit(solution)/shard_map/ppermute | solution.py:32
  278.7 3.9 %collective-permute-start.44 = (f32[1,16,32]{2,1,0:T(8,128)S(1)}, f32[1,16,32]{2,1,0:T(8,128)S(1)}, u32[]{:S(2)}, u32[]{:S(2)}) collective-permute-start(f32[1,16,32]{2,1,0:T(8,128)S(1)} %get-tuple-element.162), channel_id=1, source_target_pairs={{0,4},{4,8},{8,12},{12,16},{16,20},{20,24},{24,28},{1,5},{5,9},{9,... | collective-permute-start | bytes 6152 | tf_op jit(solution)/shard_map/ppermute | solution.py:32
  287.4 3.9 %collective-permute-start.46 = (f32[1,16,32]{2,1,0:T(8,128)S(1)}, f32[1,16,32]{2,1,0:T(8,128)S(1)}, u32[]{:S(2)}, u32[]{:S(2)}) collective-permute-start(f32[1,16,32]{2,1,0:T(8,128)S(1)} %get-tuple-element.160), channel_id=1, source_target_pairs={{0,4},{4,8},{8,12},{12,16},{16,20},{20,24},{24,28},{1,5},{5,9},{9,... | collective-permute-start | bytes 6152 | tf_op jit(solution)/shard_map/ppermute | solution.py:32
  296.2 3.9 %collective-permute-start.47 = (f32[1,1,8,64]{3,2,1,0:T(8,128)S(1)}, f32[1,1,8,64]{3,2,1,0:T(8,128)S(1)}, u32[]{:S(2)}, u32[]{:S(2)}) collective-permute-start(f32[1,1,8,64]{3,2,1,0:T(8,128)S(1)} %get-tuple-element.152), channel_id=1, source_target_pairs={{0,4},{4,8},{8,12},{12,16},{16,20},{20,24},{24,28},{1,5},{5,9},{9,... | collective-permute-start | bytes 6152 | tf_op jit(solution)/shard_map/ppermute | solution.py:32
  311.8 3.9 %collective-permute-start.51 = (f32[1,1,8,64]{3,2,1,0:T(8,128)S(1)}, f32[1,1,8,64]{3,2,1,0:T(8,128)S(1)}, u32[]{:S(2)}, u32[]{:S(2)}) collective-permute-start(f32[1,1,8,64]{3,2,1,0:T(8,128)S(1)} %get-tuple-element.150), channel_id=1, source_target_pairs={{0,4},{4,8},{8,12},{12,16},{16,20},{20,24},{24,28},{1,5},{5,9},{9,... | collective-permute-start | bytes 6152 | tf_op jit(solution)/shard_map/ppermute | solution.py:32
  327.4 3.9 collective-permute-start.55
  343.9 3.9 %collective-permute-start.59 = (f32[1,1,16,128]{3,2,1,0:T(8,128)S(1)}, f32[1,1,16,128]{3,2,1,0:T(8,128)S(1)}, u32[]{:S(2)}, u32[]{:S(2)}) collective-permute-start(f32[1,1,16,128]{3,2,1,0:T(8,128)S(1)} %get-tuple-element.102), channel_id=1, source_target_pairs={{0,4},{4,8},{8,12},{12,16},{16,20},{20,24},{24,28},{1,5},{5,9},{9,... | collective-permute-start | bytes 24584 | tf_op jit(solution)/shard_map/ppermute | solution.py:32
  359.7 3.9 %collective-permute-start.63 = (f32[1,1,16,128]{3,2,1,0:T(8,128)S(1)}, f32[1,1,16,128]{3,2,1,0:T(8,128)S(1)}, u32[]{:S(2)}, u32[]{:S(2)}) collective-permute-start(f32[1,1,16,128]{3,2,1,0:T(8,128)S(1)} %get-tuple-element.100), channel_id=1, source_target_pairs={{0,4},{4,8},{8,12},{12,16},{16,20},{20,24},{24,28},{1,5},{5,9},{9,... | collective-permute-start | bytes 24584 | tf_op jit(solution)/shard_map/ppermute | solution.py:32
  375.5 3.9 %collective-permute-start.67 = (f32[1,1,16,128]{3,2,1,0:T(8,128)S(1)}, f32[1,1,16,128]{3,2,1,0:T(8,128)S(1)}, u32[]{:S(2)}, u32[]{:S(2)}) collective-permute-start(f32[1,1,16,128]{3,2,1,0:T(8,128)S(1)} %get-tuple-element.98), channel_id=1, source_target_pairs={{0,4},{4,8},{8,12},{12,16},{16,20},{20,24},{24,28},{1,5},{5,9},{9,... | collective-permute-start | bytes 24584 | tf_op jit(solution)/shard_map/ppermute | solution.py:32
  (315 shorter events, 237.9 us)
Async XLA Ops:
  32.1 7.1 %collective-permute-start.1 = (f32[4,4,16,128]{3,2,1,0:T(8,128)S(1)}, f32[4,4,16,128]{3,2,1,0:T(8,128)S(1)}, u32[]{:S(2)}, u32[]{:S(2)}) collective-permute-start(f32[4,4,16,128]{3,2,1,0:T(8,128)S(1)} %get-tuple-element.51), channel_id=1, source_target_pairs={{4,0},{8,4},{12,8},{16,12},{20,16},{24,20},{28,24},{5,1},{9,5},{13... | collective-permute-start | bytes 393224 | tf_op jit(solution)/shard_map/ppermute | solution.py:34
  35.4 7.8 %collective-permute-start = (f32[4,4,16,128]{3,2,1,0:T(8,128)S(1)}, f32[4,4,16,128]{3,2,1,0:T(8,128)S(1)}, u32[]{:S(2)}, u32[]{:S(2)}) collective-permute-start(f32[4,4,16,128]{3,2,1,0:T(8,128)S(1)} %get-tuple-element.50), channel_id=1, source_target_pairs={{0,4},{4,8},{8,12},{12,16},{16,20},{20,24},{24,28},{1,5},{5,9},{9,... | collective-permute-start | bytes 393224 | tf_op jit(solution)/shard_map/ppermute | solution.py:32
  45.2 7.0 %collective-permute-start.2 = (f32[4,24,4,128]{3,1,2,0:T(8,128)S(1)}, f32[4,24,4,128]{3,1,2,0:T(8,128)S(1)}, u32[]{:S(2)}, u32[]{:S(2)}) collective-permute-start(f32[4,24,4,128]{3,1,2,0:T(8,128)S(1)} %copy.630), channel_id=1, source_target_pairs={{0,1},{1,2},{2,3},{4,5},{5,6},{6,7},{8,9},{9,10},{10,11},{12,13},{... | collective-permute-start | bytes 589832 | tf_op jit(solution)/shard_map/ppermute | solution.py:32
  56.8 6.4 %collective-permute-start.4 = (f32[1,1,16,128]{3,2,1,0:T(8,128)S(1)}, f32[1,1,16,128]{3,2,1,0:T(8,128)S(1)}, u32[]{:S(2)}, u32[]{:S(2)}) collective-permute-start(f32[1,1,16,128]{3,2,1,0:T(8,128)S(1)} %get-tuple-element.108), channel_id=1, source_target_pairs={{0,4},{4,8},{8,12},{12,16},{16,20},{20,24},{24,28},{1,5},{5,9},{9,... | collective-permute-start | bytes 24584 | tf_op jit(solution)/shard_map/ppermute | solution.py:32
  70.7 54.6 %collective-permute-start.9 = (f32[1,1,16,128]{3,2,1,0:T(8,128)S(1)}, f32[1,1,16,128]{3,2,1,0:T(8,128)S(1)}, u32[]{:S(2)}, u32[]{:S(2)}) collective-permute-start(f32[1,1,16,128]{3,2,1,0:T(8,128)S(1)} %get-tuple-element.107), channel_id=1, source_target_pairs={{4,0},{8,4},{12,8},{16,12},{20,16},{24,20},{28,24},{5,1},{9,5},{13... | collective-permute-start | bytes 24584 | tf_op jit(solution)/shard_map/ppermute | solution.py:34
  72.6 52.7 %collective-permute-start.8 = (f32[1,1,16,128]{3,2,1,0:T(8,128)S(1)}, f32[1,1,16,128]{3,2,1,0:T(8,128)S(1)}, u32[]{:S(2)}, u32[]{:S(2)}) collective-permute-start(f32[1,1,16,128]{3,2,1,0:T(8,128)S(1)} %get-tuple-element.106), channel_id=1, source_target_pairs={{0,4},{4,8},{8,12},{12,16},{16,20},{20,24},{24,28},{1,5},{5,9},{9,... | collective-permute-start | bytes 24584 | tf_op jit(solution)/shard_map/ppermute | solution.py:32
  135.5 6.4 %collective-permute-start.12 = (f32[1,1,16,128]{3,2,1,0:T(8,128)S(1)}, f32[1,1,16,128]{3,2,1,0:T(8,128)S(1)}, u32[]{:S(2)}, u32[]{:S(2)}) collective-permute-start(f32[1,1,16,128]{3,2,1,0:T(8,128)S(1)} %get-tuple-element.104), channel_id=1, source_target_pairs={{0,4},{4,8},{8,12},{12,16},{16,20},{20,24},{24,28},{1,5},{5,9},{9,... | collective-permute-start | bytes 24584 | tf_op jit(solution)/shard_map/ppermute | solution.py:32
  142.0 13.3 %collective-permute-start.15 = (f32[1,18,1,128]{3,2,1,0:T(1,128)S(1)}, f32[1,18,1,128]{3,2,1,0:T(1,128)S(1)}, u32[]{:S(2)}, u32[]{:S(2)}) collective-permute-start(f32[1,18,1,128]{3,2,1,0:T(1,128)S(1)} %get-tuple-element.93), channel_id=1, source_target_pairs={{1,0},{2,1},{3,2},{5,4},{6,5},{7,6},{9,8},{10,9},{11,10},{13,12},{... | collective-permute-start | bytes 27656 | tf_op jit(solution)/shard_map/ppermute | solution.py:34
  143.9 11.4 %collective-permute-start.14 = (f32[1,18,1,128]{3,2,1,0:T(1,128)S(1)}, f32[1,18,1,128]{3,2,1,0:T(1,128)S(1)}, u32[]{:S(2)}, u32[]{:S(2)}) collective-permute-start(f32[1,18,1,128]{3,2,1,0:T(1,128)S(1)} %get-tuple-element.92), channel_id=1, source_target_pairs={{0,1},{1,2},{2,3},{4,5},{5,6},{6,7},{8,9},{9,10},{10,11},{12,13},{... | collective-permute-start | bytes 27656 | tf_op jit(solution)/shard_map/ppermute | solution.py:32
  175.5 8.2 %collective-permute-start.28 = (f32[4,6,4,32]{3,2,1,0:T(4,128)S(1)}, f32[4,6,4,32]{3,2,1,0:T(4,128)S(1)}, u32[]{:S(2)}, u32[]{:S(2)}) collective-permute-start(f32[4,6,4,32]{3,2,1,0:T(4,128)S(1)} %get-tuple-element.135), channel_id=1, source_target_pairs={{0,1},{1,2},{2,3},{3,0},{4,5},{5,6},{6,7},{7,4},{8,9},{9,10},{10,1... | collective-permute-start | bytes 36872 | tf_op jit(solution)/shard_map/ppermute | solution.py:191
  182.4 8.7 %collective-permute-start.30 = (f32[4,6,4,32]{3,2,1,0:T(4,128)S(1)}, f32[4,6,4,32]{3,2,1,0:T(4,128)S(1)}, u32[]{:S(2)}, u32[]{:S(2)}) collective-permute-start(f32[4,6,4,32]{3,2,1,0:T(4,128)S(1)} %get-tuple-element.135), channel_id=1, source_target_pairs={{1,0},{2,1},{3,2},{0,3},{5,4},{6,5},{7,6},{4,7},{9,8},{10,9},{11,1... | collective-permute-start | bytes 36872 | tf_op jit(solution)/shard_map/ppermute | solution.py:193
  183.8 7.4 %collective-permute-start.29 = (f32[4,6,4,32]{3,2,1,0:T(4,128)S(1)}, f32[4,6,4,32]{3,2,1,0:T(4,128)S(1)}, u32[]{:S(2)}, u32[]{:S(2)}) collective-permute-start(f32[4,6,4,32]{3,2,1,0:T(4,128)S(1)} %collective-permute-done.28), channel_id=1, source_target_pairs={{0,1},{1,2},{2,3},{3,0},{4,5},{5,6},{6,7},{7,4},{8,9},{9,10},{10,1... | collective-permute-start | bytes 36872 | tf_op jit(solution)/shard_map/ppermute | solution.py:191
  185.3 6.7 %collective-permute-start.21 = (f32[1,1,8,64]{3,2,1,0:T(8,128)S(1)}, f32[1,1,8,64]{3,2,1,0:T(8,128)S(1)}, u32[]{:S(2)}, u32[]{:S(2)}) collective-permute-start(f32[1,1,8,64]{3,2,1,0:T(8,128)S(1)} %get-tuple-element.201), channel_id=1, source_target_pairs={{4,0},{8,4},{12,8},{16,12},{20,16},{24,20},{28,24},{5,1},{9,5},{13... | collective-permute-start | bytes 6152 | tf_op jit(solution)/shard_map/ppermute | solution.py:34
  226.8 6.4 %collective-permute-start.32 = (f32[1,16,32]{2,1,0:T(8,128)S(1)}, f32[1,16,32]{2,1,0:T(8,128)S(1)}, u32[]{:S(2)}, u32[]{:S(2)}) collective-permute-start(f32[1,16,32]{2,1,0:T(8,128)S(1)} %broadcast_in_dim.286), channel_id=1, source_target_pairs={{0,4},{4,8},{8,12},{12,16},{16,20},{20,24},{24,28},{1,5},{5,9},{9,... | collective-permute-start | bytes 6152 | tf_op jit(solution)/shard_map/ppermute | solution.py:32
  235.7 6.4 %collective-permute-start.34 = (f32[1,16,32]{2,1,0:T(8,128)S(1)}, f32[1,16,32]{2,1,0:T(8,128)S(1)}, u32[]{:S(2)}, u32[]{:S(2)}) collective-permute-start(f32[1,16,32]{2,1,0:T(8,128)S(1)} %get-tuple-element.192), channel_id=1, source_target_pairs={{0,4},{4,8},{8,12},{12,16},{16,20},{20,24},{24,28},{1,5},{5,9},{9,... | collective-permute-start | bytes 6152 | tf_op jit(solution)/shard_map/ppermute | solution.py:32
  244.4 6.4 %collective-permute-start.36 = (f32[1,16,32]{2,1,0:T(8,128)S(1)}, f32[1,16,32]{2,1,0:T(8,128)S(1)}, u32[]{:S(2)}, u32[]{:S(2)}) collective-permute-start(f32[1,16,32]{2,1,0:T(8,128)S(1)} %get-tuple-element.186), channel_id=1, source_target_pairs={{0,4},{4,8},{8,12},{12,16},{16,20},{20,24},{24,28},{1,5},{5,9},{9,... | collective-permute-start | bytes 6152 | tf_op jit(solution)/shard_map/ppermute | solution.py:32
  253.0 6.4 %collective-permute-start.38 = (f32[1,16,32]{2,1,0:T(8,128)S(1)}, f32[1,16,32]{2,1,0:T(8,128)S(1)}, u32[]{:S(2)}, u32[]{:S(2)}) collective-permute-start(f32[1,16,32]{2,1,0:T(8,128)S(1)} %get-tuple-element.180), channel_id=1, source_target_pairs={{0,4},{4,8},{8,12},{12,16},{16,20},{20,24},{24,28},{1,5},{5,9},{9,... | collective-permute-start | bytes 6152 | tf_op jit(solution)/shard_map/ppermute | solution.py:32
  261.6 6.4 %collective-permute-start.40 = (f32[1,16,32]{2,1,0:T(8,128)S(1)}, f32[1,16,32]{2,1,0:T(8,128)S(1)}, u32[]{:S(2)}, u32[]{:S(2)}) collective-permute-start(f32[1,16,32]{2,1,0:T(8,128)S(1)} %get-tuple-element.174), channel_id=1, source_target_pairs={{0,4},{4,8},{8,12},{12,16},{16,20},{20,24},{24,28},{1,5},{5,9},{9,... | collective-permute-start | bytes 6152 | tf_op jit(solution)/shard_map/ppermute | solution.py:32
  270.1 6.4 %collective-permute-start.42 = (f32[1,16,32]{2,1,0:T(8,128)S(1)}, f32[1,16,32]{2,1,0:T(8,128)S(1)}, u32[]{:S(2)}, u32[]{:S(2)}) collective-permute-start(f32[1,16,32]{2,1,0:T(8,128)S(1)} %get-tuple-element.168), channel_id=1, source_target_pairs={{0,4},{4,8},{8,12},{12,16},{16,20},{20,24},{24,28},{1,5},{5,9},{9,... | collective-permute-start | bytes 6152 | tf_op jit(solution)/shard_map/ppermute | solution.py:32
  278.7 6.4 %collective-permute-start.44 = (f32[1,16,32]{2,1,0:T(8,128)S(1)}, f32[1,16,32]{2,1,0:T(8,128)S(1)}, u32[]{:S(2)}, u32[]{:S(2)}) collective-permute-start(f32[1,16,32]{2,1,0:T(8,128)S(1)} %get-tuple-element.162), channel_id=1, source_target_pairs={{0,4},{4,8},{8,12},{12,16},{16,20},{20,24},{24,28},{1,5},{5,9},{9,... | collective-permute-start | bytes 6152 | tf_op jit(solution)/shard_map/ppermute | solution.py:32
  287.4 6.4 %collective-permute-start.46 = (f32[1,16,32]{2,1,0:T(8,128)S(1)}, f32[1,16,32]{2,1,0:T(8,128)S(1)}, u32[]{:S(2)}, u32[]{:S(2)}) collective-permute-start(f32[1,16,32]{2,1,0:T(8,128)S(1)} %get-tuple-element.160), channel_id=1, source_target_pairs={{0,4},{4,8},{8,12},{12,16},{16,20},{20,24},{24,28},{1,5},{5,9},{9,... | collective-permute-start | bytes 6152 | tf_op jit(solution)/shard_map/ppermute | solution.py:32
  343.9 6.4 %collective-permute-start.59 = (f32[1,1,16,128]{3,2,1,0:T(8,128)S(1)}, f32[1,1,16,128]{3,2,1,0:T(8,128)S(1)}, u32[]{:S(2)}, u32[]{:S(2)}) collective-permute-start(f32[1,1,16,128]{3,2,1,0:T(8,128)S(1)} %get-tuple-element.102), channel_id=1, source_target_pairs={{0,4},{4,8},{8,12},{12,16},{16,20},{20,24},{24,28},{1,5},{5,9},{9,... | collective-permute-start | bytes 24584 | tf_op jit(solution)/shard_map/ppermute | solution.py:32
  359.7 6.4 %collective-permute-start.63 = (f32[1,1,16,128]{3,2,1,0:T(8,128)S(1)}, f32[1,1,16,128]{3,2,1,0:T(8,128)S(1)}, u32[]{:S(2)}, u32[]{:S(2)}) collective-permute-start(f32[1,1,16,128]{3,2,1,0:T(8,128)S(1)} %get-tuple-element.100), channel_id=1, source_target_pairs={{0,4},{4,8},{8,12},{12,16},{16,20},{20,24},{24,28},{1,5},{5,9},{9,... | collective-permute-start | bytes 24584 | tf_op jit(solution)/shard_map/ppermute | solution.py:32
  375.5 6.4 %collective-permute-start.67 = (f32[1,1,16,128]{3,2,1,0:T(8,128)S(1)}, f32[1,1,16,128]{3,2,1,0:T(8,128)S(1)}, u32[]{:S(2)}, u32[]{:S(2)}) collective-permute-start(f32[1,1,16,128]{3,2,1,0:T(8,128)S(1)} %get-tuple-element.98), channel_id=1, source_target_pairs={{0,4},{4,8},{8,12},{12,16},{16,20},{20,24},{24,28},{1,5},{5,9},{9,... | collective-permute-start | bytes 24584 | tf_op jit(solution)/shard_map/ppermute | solution.py:32
  (49 other events, 276.3 us)
